TPU v7x, 512 devices: a whole 4x4x16 slice. The times are simulated.
512 devices in a mesh: tm: 128 (over z, y, core), chan: 4 (over x).
Axes of the slice: x: 4, y: 4, z: 16, core: 2. Of those that a mesh axis runs over, the one named last changes fastest.
Arguments:
- series: bfloat16 [32768, 512], P('tm', 'chan'), may hold values from -6 to 6
- proj_weight: bfloat16 [512, 3, 512], P(None, None, 'chan'), may hold values from -0.25 to 0.25
- proj_bias: float32 [3, 512], P(None, 'chan'), may hold values from -6 to 6
- short_taps: float32 [3, 3, 512], P(None, None, 'chan'), may hold values from -6 to 6
- short_bias: float32 [3, 512], P(None, 'chan'), may hold values from -6 to 6
- spectrum: float32 [2, 128, 2, 256, 512], P(None, 'tm', None, None, 'chan'), may hold values from -6 to 6
- skip_gain: float32 [512], P('chan'), may hold values from -6 to 6
- out_weight: bfloat16 [512, 512], replicated, may hold values from -0.25 to 0.25
- out_bias: float32 [512], P('chan'), may hold values from -6 to 6
Outputs:
- mixed_out: bfloat16 [32768, 512], P('tm', 'chan')
All inputs are finite; a program needn't handle non-finite values.
Results may differ from a plain program's by a relative error of at most 0.009.
Values may be sent and summed in bfloat16 or wider, within the bound.
No kernel may reach another device: no remote copies, remote signals or barrier semaphores. Data moves between devices by JAX's collectives and lax.ppermute only.
A program may use at most 64 MiB of HBM per device.

v0:
```python
import math
import jax
import jax.numpy as jnp
import numpy as np
from jax import lax
from jax.sharding import PartitionSpec as P

HI = lax.Precision.HIGHEST


def from_behind(array, axis, by):
    length = lax.axis_size(axis)
    pairs = [(i, i + by) for i in range(length) if 0 <= i + by < length]
    return lax.ppermute(array, axis, pairs)


def reverse_bits_np(values, digits):
    result = np.zeros_like(values)
    for bit_level in range(digits):
        result = result | (values >> bit_level & 1) << digits - 1 - bit_level
    return result


def dft_tables(tm_count, steps_dev):
    rows = 2 * tm_count
    digits = tm_count.bit_length() - 1
    r = np.arange(rows)
    k1 = 2 * reverse_bits_np(r // 2, digits) + r % 2
    m = np.arange(tm_count)
    t = np.arange(steps_dev)
    b = np.arange(steps_dev)
    period = rows * steps_dev
    ang1 = 2 * np.pi * (k1[:, None] * m[None, :] % rows) / rows
    ang2 = 2 * np.pi * (t[:, None] * b[None, :] % steps_dev) / steps_dev
    angt = 2 * np.pi * (k1[:, None] * t[None, :] % period) / period
    f32 = lambda a: jnp.asarray(a.astype(np.float32))
    return dict(
        c1=f32(np.cos(ang1)),
        s1=f32(np.sin(ang1)),
        c2=f32(np.cos(ang2)),
        s2=f32(np.sin(ang2)),
        ct=f32(np.cos(angt)),
        st=f32(np.sin(angt)),
        period=period,
    )


def mm(a, b):
    return jnp.dot(a, b, precision=HI, preferred_element_type=jnp.float32)


def long_conv(x, h, tab):
    c1, s1, c2, s2, ct, st = (tab[k] for k in ("c1", "s1", "c2", "s2", "ct", "st"))
    ar = mm(c1, x)
    ai = -mm(s1, x)
    tr = ar * ct + ai * st
    ti = ai * ct - ar * st
    zr = mm(tr, c2) + mm(ti, s2)
    zi = mm(ti, c2) - mm(tr, s2)
    yr = h[0] * zr - h[1] * zi
    yi = h[0] * zi + h[1] * zr
    br = mm(yr, c2) - mm(yi, s2)
    bi = mm(yi, c2) + mm(yr, s2)
    ur = br * ct - bi * st
    ui = bi * ct + br * st
    y = lax.dot_general(
        c1, ur, (((0,), (0,)), ((), ())), precision=HI, preferred_element_type=jnp.float32
    )
    y = y - lax.dot_general(
        s1, ui, (((0,), (0,)), ((), ())), precision=HI, preferred_element_type=jnp.float32
    )
    return y * (1.0 / tab["period"])


def shards(
    series,
    proj_weight,
    proj_bias,
    short_taps,
    short_bias,
    spectrum,
    skip_gain,
    out_weight,
    out_bias,
):
    steps_dev = series.shape[0]
    model_width = proj_weight.shape[0]
    channels = proj_weight.shape[2]
    tm_count = lax.axis_size("tm")
    tab = dft_tables(tm_count, steps_dev)
    flat_weight = proj_weight.reshape(model_width, 3 * channels)
    projected = jnp.dot(
        lax.all_gather(series, "chan", axis=1, tiled=True),
        flat_weight,
        preferred_element_type=jnp.float32,
    )
    projected = (projected.reshape(steps_dev, 3, channels) + proj_bias).astype(jnp.bfloat16)
    taps_count = short_taps.shape[0]
    earlier = from_behind(projected[steps_dev - taps_count + 1 :], "tm", 1)
    extended = jnp.concatenate([earlier, projected], 0).astype(jnp.float32)
    streams = short_bias + short_taps[0] * extended[taps_count - 1 :]
    for offset in range(1, taps_count):
        streams = (
            streams
            + short_taps[offset]
            * extended[taps_count - 1 - offset : taps_count - 1 - offset + steps_dev]
        )
    streams = streams.astype(jnp.bfloat16)
    gate_out = streams[:, 0]
    mixed_in = (streams[:, 1].astype(jnp.float32) * streams[:, 2].astype(jnp.float32)).astype(
        jnp.bfloat16
    )
    pair = jnp.stack([mixed_in, gate_out])[:, None]
    pair = lax.all_to_all(pair, "tm", 3, 1, tiled=True)
    signal_bf = pair[0, :, :, 0]
    gate_own = pair[1, :, :, 0].astype(jnp.float32)
    h = lax.all_to_all(spectrum, "tm", 4, 1, tiled=True)
    h = h.reshape(2, 2 * tm_count, steps_dev)
    signal = signal_bf.astype(jnp.float32)
    convolved = long_conv(signal, h, tab)
    skip = lax.dynamic_index_in_dim(skip_gain, lax.axis_index("tm"), 0, keepdims=False)
    gated = ((convolved + skip * signal) * gate_own).astype(jnp.bfloat16)
    gated = lax.all_to_all(gated[:, :, None], "tm", 0, 2, tiled=True)
    gated = lax.all_gather(gated[0], "chan", axis=1, tiled=True)
    column_start = lax.axis_index("chan") * channels
    weight_cols = lax.dynamic_slice_in_dim(out_weight, column_start, channels, 1)
    mixed_out = jnp.dot(gated, weight_cols, preferred_element_type=jnp.float32) + out_bias
    return mixed_out.astype(jnp.bfloat16)


def solution(mesh):
    return jax.shard_map(
        shards,
        mesh=mesh,
        in_specs=(
            P("tm", "chan"),
            P(None, None, "chan"),
            P(None, "chan"),
            P(None, None, "chan"),
            P(None, "chan"),
            P(None, "tm", None, None, "chan"),
            P("chan"),
            P(),
            P("chan"),
        ),
        out_specs=P("tm", "chan"),
        check_vma=False,
    )
```

profile of v0, /device:TPU:2, one launch (start us, length us, event | category | flops | bytes accessed | tf_op | source)
XLA Modules:
  0.0 140.7 jit_solution(8496077110473266639)
XLA Ops:
  0.0 1.2 copy.32
  1.3 15.2 %all_gather.6 = bf16[256,512]{1,0:T(8,128)(2,1)S(1)} all-gather(bf16[256,128]{1,0:T(8,128)(2,1)S(1)} %copy-done.13), channel_id=1, replica_groups=mesh['tm'=128,'chan'=4] {'chan'}, dimensions={1}, use_global_device_ids=true | all-gather | bytes 327680 | tf_op jit(solution)/shard_map/all_gather | solution.py:93
  16.8 1.3 collective-permute-start
  18.1 0.8 collective-permute-done
  18.9 0.7 copy-done.16
  19.8 0.8 copy.33
  20.6 20.5 %all-to-all-start.1 = ((bf16[2,1,256,128]{2,0,1,3:T(2,128)(2,1)}), bf16[2,1,256,128]{2,0,1,3:T(2,128)(2,1)S(1)}, u32[]{:S(2)}, u32[]{:S(2)}) async-start(bf16[2,1,256,128]{2,0,1,3:T(2,128)(2,1)} %copy.33), calls=%async_computation.1 | async-start | bytes 262144 | tf_op jit(solution)/shard_map/all_to_all | solution.py:114
  41.1 1.0 copy.31
  42.1 14.4 %all-to-all-done.1 = bf16[2,1,256,128]{2,0,1,3:T(2,128)(2,1)S(1)} async-done(((bf16[2,1,256,128]{2,0,1,3:T(2,128)(2,1)}), bf16[2,1,256,128]{2,0,1,3:T(2,128)(2,1)S(1)}, u32[]{:S(2)}, u32[]{:S(2)}) %all-to-all-start.1) | async-done | bytes 131104 | tf_op jit(solution)/shard_map/all_to_all | solution.py:114
  56.5 7.8 %all-to-all-start = ((f32[2,1,2,256,128]{3,2,1,0,4:T(2,128)}), f32[2,1,2,256,128]{3,2,1,0,4:T(2,128)S(1)}, u32[]{:S(2)}, u32[]{:S(2)}) async-start(f32[2,1,2,256,128]{3,2,1,0,4:T(2,128)} %copy.31), calls=%async_computation | async-start | bytes 1048576 | tf_op jit(solution)/shard_map/all_to_all | solution.py:117
  64.4 0.6 copy-done.18
  65.0 0.6 dynamic_slice.7
  65.7 0.8 copy-done.11
  67.8 0.4 fusion.23
  68.2 0.6 copy-done.1
  68.8 1.1 fusion.24
  69.9 0.4 convolution_add_fusion.2
  70.3 24.9 %all-to-all-done = f32[2,1,2,256,128]{3,2,1,0,4:T(2,128)S(1)} async-done(((f32[2,1,2,256,128]{3,2,1,0,4:T(2,128)}), f32[2,1,2,256,128]{3,2,1,0,4:T(2,128)S(1)}, u32[]{:S(2)}, u32[]{:S(2)}) %all-to-all-start) | async-done | bytes 524320 | tf_op jit(solution)/shard_map/all_to_all | solution.py:117
  95.8 0.8 copy-done.7
  96.6 1.4 multiply_subtract_fusion
  98.7 0.4 convolution_add_fusion.1
  99.1 0.4 convolution_subtract_fusion
  99.5 0.5 copy-done.9
  100.0 0.6 fusion.18
  100.9 1.2 fusion.7
  102.3 0.5 broadcast.5
  102.8 1.0 reduce
  103.8 0.7 reshape.55
  104.5 9.0 %all-to-all-start.2 = ((bf16[128,2,128]{2,1,0:T(2,128)(2,1)}), bf16[128,2,128]{2,1,0:T(2,128)(2,1)S(1)}, u32[]{:S(2)}, u32[]{:S(2)}) async-start(bf16[128,2,128]{2,1,0:T(2,128)(2,1)} %reshape.55), calls=%async_computation.2 | async-start | bytes 131072 | tf_op jit(solution)/shard_map/all_to_all | solution.py:123
  113.5 14.5 %all-to-all-done.2 = bf16[128,2,128]{2,1,0:T(2,128)(2,1)S(1)} async-done(((bf16[128,2,128]{2,1,0:T(2,128)(2,1)}), bf16[128,2,128]{2,1,0:T(2,128)(2,1)S(1)}, u32[]{:S(2)}, u32[]{:S(2)}) %all-to-all-start.2) | async-done | bytes 65568 | tf_op jit(solution)/shard_map/all_to_all | solution.py:123
  128.0 11.8 %all-gather = bf16[1,256,512,1]{1,2,3,0:T(8,128)(2,1)S(1)} all-gather(bf16[1,256,128,1]{1,2,3,0:T(8,128)(2,1)S(1)} %bitcast.98), channel_id=2, replica_groups=mesh['tm'=128,'chan'=4] {'chan'}, dimensions={2}, use_global_device_ids=true | all-gather | bytes 327680 | tf_op jit(solution)/shard_map/all_gather | solution.py:124
  139.8 0.9 fusion.6
  (51 shorter events, 3.9 us)
Async XLA Ops:
  0.0 139.8 %copy-start = (bf16[512,512]{1,0:T(8,128)(2,1)S(1)}, bf16[512,512]{1,0:T(8,128)(2,1)}, u32[]{:S(2)}) copy-start(bf16[512,512]{1,0:T(8,128)(2,1)} %param.22) | copy-start | bytes 1572868
  0.0 1.2 copy-start.13
  1.2 15.2 %copy-start.15 = (f32[3,128]{1,0:T(4,128)S(1)}, f32[3,128]{1,0:T(4,128)}, u32[]{:S(2)}) copy-start(f32[3,128]{1,0:T(4,128)} %param.17) | copy-start | bytes 4612
  16.4 1.6 %copy-start.14 = (f32[3,3,128]{2,1,0:T(4,128)S(1)}, f32[3,3,128]{2,1,0:T(4,128)}, u32[]{:S(2)}) copy-start(f32[3,3,128]{2,1,0:T(4,128)} %param.18) | copy-start | bytes 13828
  16.8 2.1 %collective-permute-start = (bf16[2,3,128]{2,0,1:T(2,128)(2,1)S(1)}, bf16[2,3,128]{2,0,1:T(2,128)(2,1)S(1)}, u32[]{:S(2)}, u32[]{:S(2)}) collective-permute-start(bf16[2,3,128]{2,0,1:T(2,128)(2,1)S(1)} %slice.63), channel_id=1, source_target_pairs={{0,4},{4,8},{8,12},{12,16},{16,20},{20,24},{24,28},{28,32},{32,36}... | collective-permute-start | bytes 4616 | tf_op jit(solution)/shard_map/ppermute | solution.py:14
  18.9 0.7 copy-start.16
  19.8 21.4 %copy-start.10 = (f32[2,1,2,256,128]{4,3,2,1,0:T(8,128)S(1)}, f32[2,1,2,256,128]{4,3,2,1,0:T(8,128)}, u32[]{:S(2)}) copy-start(f32[2,1,2,256,128]{4,3,2,1,0:T(8,128)} %param.20) | copy-start | bytes 1572868
  20.6 35.9 %all-to-all-start.1 = ((bf16[2,1,256,128]{2,0,1,3:T(2,128)(2,1)}), bf16[2,1,256,128]{2,0,1,3:T(2,128)(2,1)S(1)}, u32[]{:S(2)}, u32[]{:S(2)}) async-start(bf16[2,1,256,128]{2,0,1,3:T(2,128)(2,1)} %copy.33), calls=%async_computation.1 | async-start | bytes 262144 | tf_op jit(solution)/shard_map/all_to_all | solution.py:114
  56.5 38.7 %all-to-all-start = ((f32[2,1,2,256,128]{3,2,1,0,4:T(2,128)}), f32[2,1,2,256,128]{3,2,1,0,4:T(2,128)S(1)}, u32[]{:S(2)}, u32[]{:S(2)}) async-start(f32[2,1,2,256,128]{3,2,1,0,4:T(2,128)} %copy.31), calls=%async_computation | async-start | bytes 1048576 | tf_op jit(solution)/shard_map/all_to_all | solution.py:117
  64.3 0.7 copy-start.18
  65.6 0.9 copy-start.11
  65.6 1.2 copy-start.8
  66.5 1.0 copy-start.3
  66.5 1.0 copy-start.6
  66.8 1.0 copy-start.2
  67.8 0.9 copy-start.1
  67.8 1.0 copy-start.5
  68.8 1.1 copy-start.4
  95.6 1.0 copy-start.7
  99.1 0.9 copy-start.9
  100.0 0.9 copy-start.12
  104.5 23.5 %all-to-all-start.2 = ((bf16[128,2,128]{2,1,0:T(2,128)(2,1)}), bf16[128,2,128]{2,1,0:T(2,128)(2,1)S(1)}, u32[]{:S(2)}, u32[]{:S(2)}) async-start(bf16[128,2,128]{2,1,0:T(2,128)(2,1)} %reshape.55), calls=%async_computation.2 | async-start | bytes 131072 | tf_op jit(solution)/shard_map/all_to_all | solution.py:123
  128.0 11.8 %copy-start.17 = (f32[128]{0:T(128)S(1)}, f32[128]{0:T(128)}, u32[]{:S(2)}) copy-start(f32[128]{0:T(128)} %param.23) | copy-start | bytes 1540
where the time goes:
time: 141 us
  waiting for transfers between devices  54.5 us (39%)
  starting transfers between devices  38.6 us (27%)
  blocking collectives  26.9 us (19%)
  local copies, waits for them, and re-layouts  10.7 us (8%)
  matrix products  8.38 us (6%)
    all_to_all x1, waiting for transfers between devices, shards(): h = lax.all_to_all(spectrum, 'tm', 4, 1, tiled=True)  24.9 us
    all_to_all x1, starting transfers between devices, shards(): pair = lax.all_to_all(pair, 'tm', 3, 1, tiled=True)  20.5 us
    all_gather x1, blocking collectives, shards(): lax.all_gather(series, 'chan', axis=1, tiled=True)  15.2 us
    all_to_all x1, waiting for transfers between devices, shards(): gated = lax.all_to_all(gated[:, :, None], 'tm', 0, 2, tiled=True)  14.5 us
    all_to_all x1, waiting for transfers between devices, shards(): pair = lax.all_to_all(pair, 'tm', 3, 1, tiled=True)  14.4 us
    all_gather x1, blocking collectives, shards(): gated = lax.all_gather(gated[0], 'chan', axis=1, tiled=True)  11.8 us
    all_to_all x1, starting transfers between devices, shards(): gated = lax.all_to_all(gated[:, :, None], 'tm', 0, 2, tiled=True)  9.02 us
    unnamed x44, local copies, waits for them, and re-layouts  8.47 us
  transfers between devices with their start and end apart: 4, of which 4 were waited for; matrix products, arithmetic and copies ran while one was open for 3% of the time, Pallas kernels for 0%

commit v1 on v0

--- a/solution.py
+++ b/solution.py
@@ -6,6 +6,27 @@
 from jax.sharding import PartitionSpec as P
 
 HI = lax.Precision.HIGHEST
+
+
+def ring_gather(value, axis, dim):
+    size, index, width = (lax.axis_size(axis), lax.axis_index(axis), value.shape[dim])
+    right = [(i, (i + 1) % size) for i in range(size)]
+    backward = [(i, (i - 1) % size) for i in range(size)]
+    out = jnp.zeros((*value.shape[:dim], size * width, *value.shape[dim + 1 :]), value.dtype)
+    out = lax.dynamic_update_slice_in_dim(out, value, index * width, axis=dim)
+    from_left = from_right = value
+    halfway = size // 2
+    for step in range(1, halfway + 1):
+        from_left = lax.ppermute(from_left, axis, right)
+        out = lax.dynamic_update_slice_in_dim(
+            out, from_left, (index - step) % size * width, axis=dim
+        )
+        if step < size - halfway:
+            from_right = lax.ppermute(from_right, axis, backward)
+            out = lax.dynamic_update_slice_in_dim(
+                out, from_right, (index + step) % size * width, axis=dim
+            )
+    return out
 
 
 def from_behind(array, axis, by):
@@ -121,7 +142,7 @@
     skip = lax.dynamic_index_in_dim(skip_gain, lax.axis_index("tm"), 0, keepdims=False)
     gated = ((convolved + skip * signal) * gate_own).astype(jnp.bfloat16)
     gated = lax.all_to_all(gated[:, :, None], "tm", 0, 2, tiled=True)
-    gated = lax.all_gather(gated[0], "chan", axis=1, tiled=True)
+    gated = ring_gather(gated[0], "chan", 1)
     column_start = lax.axis_index("chan") * channels
     weight_cols = lax.dynamic_slice_in_dim(out_weight, column_start, channels, 1)
     mixed_out = jnp.dot(gated, weight_cols, preferred_element_type=jnp.float32) + out_bias

time: 141 us -> 143 us (1.014)
  the two profiles are of different devices: /device:TPU:2 before, /device:TPU:32 now
where the time goes in v1:
time: 143 us
  waiting for transfers between devices  67.7 us (47%)
  starting transfers between devices  42 us (29%)
  blocking collectives  12 us (8%)
  local copies, waits for them, and re-layouts  10.7 us (7%)
  matrix products  8.41 us (6%)
    all_to_all x1, waiting for transfers between devices, shards(): h = lax.all_to_all(spectrum, 'tm', 4, 1, tiled=True)  27.1 us
    all_to_all x1, starting transfers between devices, shards(): pair = lax.all_to_all(pair, 'tm', 3, 1, tiled=True)  17.7 us
    all_to_all x1, waiting for transfers between devices, shards(): pair = lax.all_to_all(pair, 'tm', 3, 1, tiled=True)  16.1 us
    all_to_all x1, waiting for transfers between devices, shards(): gated = lax.all_to_all(gated[:, :, None], 'tm', 0, 2, tiled=True)  14.3 us
    all_gather x1, blocking collectives, shards(): lax.all_gather(series, 'chan', axis=1, tiled=True)  12 us
    unnamed x43, local copies, waits for them, and re-layouts  8.48 us
    all_to_all x1, starting transfers between devices, shards(): gated = lax.all_to_all(gated[:, :, None], 'tm', 0, 2, tiled=True)  6.77 us
    all_to_all x1, starting transfers between devices, shards(): h = lax.all_to_all(spectrum, 'tm', 4, 1, tiled=True)  6.1 us
  transfers between devices with their start and end apart: 7, of which 7 were waited for; matrix products, arithmetic and copies ran while one was open for 3% of the time, Pallas kernels for 0%

profile of v1, /device:TPU:32, one launch (start us, length us, event | category | flops | bytes accessed | tf_op | source)
XLA Modules:
  0.0 142.6 jit_solution(12518707132341514371)
XLA Ops:
  0.0 1.2 copy.32
  1.3 12.0 %all_gather.3 = bf16[256,512]{1,0:T(8,128)(2,1)S(1)} all-gather(bf16[256,128]{1,0:T(8,128)(2,1)S(1)} %copy-done.13), channel_id=1, replica_groups=mesh['tm'=128,'chan'=4] {'chan'}, dimensions={1}, use_global_device_ids=true | all-gather | bytes 327680 | tf_op jit(solution)/shard_map/all_gather | solution.py:114
  13.6 1.9 %collective-permute-start = (bf16[2,3,128]{2,0,1:T(2,128)(2,1)S(1)}, bf16[2,3,128]{2,0,1:T(2,128)(2,1)S(1)}, u32[]{:S(2)}, u32[]{:S(2)}) collective-permute-start(bf16[2,3,128]{2,0,1:T(2,128)(2,1)S(1)} %slice.63), channel_id=1, source_target_pairs={{0,4},{4,8},{8,12},{12,16},{16,20},{20,24},{24,28},{28,32},{32,36}... | collective-permute-start | bytes 4616 | tf_op jit(solution)/shard_map/ppermute | solution.py:35
  15.5 5.1 %collective-permute-done = bf16[2,3,128]{2,0,1:T(2,128)(2,1)S(1)} collective-permute-done((bf16[2,3,128]{2,0,1:T(2,128)(2,1)S(1)}, bf16[2,3,128]{2,0,1:T(2,128)(2,1)S(1)}, u32[]{:S(2)}, u32[]{:S(2)}) %collective-permute-start) | collective-permute-done | bytes 1568 | tf_op jit(solution)/shard_map/ppermute | solution.py:35
  20.7 0.7 copy-done.16
  21.6 0.8 copy.33
  22.4 17.7 %all-to-all-start.1 = ((bf16[2,1,256,128]{2,0,1,3:T(2,128)(2,1)}), bf16[2,1,256,128]{2,0,1,3:T(2,128)(2,1)S(1)}, u32[]{:S(2)}, u32[]{:S(2)}) async-start(bf16[2,1,256,128]{2,0,1,3:T(2,128)(2,1)} %copy.33), calls=%async_computation.1 | async-start | bytes 262144 | tf_op jit(solution)/shard_map/all_to_all | solution.py:135
  40.1 1.0 copy.31
  41.1 16.1 %all-to-all-done.1 = bf16[2,1,256,128]{2,0,1,3:T(2,128)(2,1)S(1)} async-done(((bf16[2,1,256,128]{2,0,1,3:T(2,128)(2,1)}), bf16[2,1,256,128]{2,0,1,3:T(2,128)(2,1)S(1)}, u32[]{:S(2)}, u32[]{:S(2)}) %all-to-all-start.1) | async-done | bytes 131104 | tf_op jit(solution)/shard_map/all_to_all | solution.py:135
  57.2 6.1 %all-to-all-start = ((f32[2,1,2,256,128]{3,2,1,0,4:T(2,128)}), f32[2,1,2,256,128]{3,2,1,0,4:T(2,128)S(1)}, u32[]{:S(2)}, u32[]{:S(2)}) async-start(f32[2,1,2,256,128]{3,2,1,0,4:T(2,128)} %copy.31), calls=%async_computation | async-start | bytes 1048576 | tf_op jit(solution)/shard_map/all_to_all | solution.py:138
  63.3 0.6 copy-done.18
  64.0 0.6 dynamic_slice.7
  64.7 0.8 copy-done.11
  67.2 0.5 copy-done.1
  67.8 1.1 fusion.23
  68.9 0.4 convolution_add_fusion.2
  69.3 27.1 %all-to-all-done = f32[2,1,2,256,128]{3,2,1,0,4:T(2,128)S(1)} async-done(((f32[2,1,2,256,128]{3,2,1,0,4:T(2,128)}), f32[2,1,2,256,128]{3,2,1,0,4:T(2,128)S(1)}, u32[]{:S(2)}, u32[]{:S(2)}) %all-to-all-start) | async-done | bytes 524320 | tf_op jit(solution)/shard_map/all_to_all | solution.py:138
  97.0 0.8 copy-done.7
  97.8 1.4 multiply_subtract_fusion
  100.7 0.5 copy-done.9
  101.2 0.6 fusion.17
  102.1 1.2 fusion.7
  103.5 0.5 broadcast.8
  104.0 1.0 reduce
  105.0 0.7 reshape.54
  105.7 6.8 %all-to-all-start.2 = ((bf16[128,2,128]{2,1,0:T(2,128)(2,1)}), bf16[128,2,128]{2,1,0:T(2,128)(2,1)S(1)}, u32[]{:S(2)}, u32[]{:S(2)}) async-start(bf16[128,2,128]{2,1,0:T(2,128)(2,1)} %reshape.54), calls=%async_computation.2 | async-start | bytes 131072 | tf_op jit(solution)/shard_map/all_to_all | solution.py:144
  112.5 14.3 %all-to-all-done.2 = bf16[128,2,128]{2,1,0:T(2,128)(2,1)S(1)} async-done(((bf16[128,2,128]{2,1,0:T(2,128)(2,1)}), bf16[128,2,128]{2,1,0:T(2,128)(2,1)S(1)}, u32[]{:S(2)}, u32[]{:S(2)}) %all-to-all-start.2) | async-done | bytes 65568 | tf_op jit(solution)/shard_map/all_to_all | solution.py:144
  126.9 3.6 %collective-permute-start.1 = (bf16[256,128]{0,1:T(8,128)(2,1)S(1)}, bf16[256,128]{0,1:T(8,128)(2,1)S(1)}, u32[]{:S(2)}, u32[]{:S(2)}) collective-permute-start(bf16[256,128]{0,1:T(8,128)(2,1)S(1)} %get-tuple-element.6), channel_id=1, source_target_pairs={{0,1},{1,2},{2,3},{3,0},{4,5},{5,6},{6,7},{7,4},{8,9},{9,10},{10,1... | collective-permute-start | bytes 196616 | tf_op jit(solution)/shard_map/ppermute | solution.py:20
  130.6 3.4 %collective-permute-start.2 = (bf16[256,128]{0,1:T(8,128)(2,1)S(1)}, bf16[256,128]{0,1:T(8,128)(2,1)S(1)}, u32[]{:S(2)}, u32[]{:S(2)}) collective-permute-start(bf16[256,128]{0,1:T(8,128)(2,1)S(1)} %get-tuple-element.6), channel_id=1, source_target_pairs={{0,3},{1,0},{2,1},{3,2},{4,7},{5,4},{6,5},{7,6},{8,11},{9,8},{10,9... | collective-permute-start | bytes 196616 | tf_op jit(solution)/shard_map/ppermute | solution.py:25
  134.3 2.4 %collective-permute-start.3 = (bf16[256,128]{0,1:T(8,128)(2,1)S(1)}, bf16[256,128]{0,1:T(8,128)(2,1)S(1)}, u32[]{:S(2)}, u32[]{:S(2)}) collective-permute-start(bf16[256,128]{0,1:T(8,128)(2,1)S(1)} %collective-permute-done.1), channel_id=1, source_target_pairs={{0,1},{1,2},{2,3},{3,0},{4,5},{5,6},{6,7},{7,4},{8,9},{9,10},{10,1... | collective-permute-start | bytes 196616 | tf_op jit(solution)/shard_map/ppermute | solution.py:20
  136.8 4.9 %collective-permute-done.3 = bf16[256,128]{0,1:T(8,128)(2,1)S(1)} collective-permute-done((bf16[256,128]{0,1:T(8,128)(2,1)S(1)}, bf16[256,128]{0,1:T(8,128)(2,1)S(1)}, u32[]{:S(2)}, u32[]{:S(2)}) %collective-permute-start.3) | collective-permute-done | bytes 65568 | tf_op jit(solution)/shard_map/ppermute | solution.py:20
  141.7 0.9 fusion.6
  (60 shorter events, 5.4 us)
Async XLA Ops:
  0.0 141.6 %copy-start = (bf16[512,512]{1,0:T(8,128)(2,1)S(1)}, bf16[512,512]{1,0:T(8,128)(2,1)}, u32[]{:S(2)}) copy-start(bf16[512,512]{1,0:T(8,128)(2,1)} %param.22) | copy-start | bytes 1572868
  0.0 1.2 copy-start.13
  1.2 12.0 %copy-start.15 = (f32[3,128]{1,0:T(4,128)S(1)}, f32[3,128]{1,0:T(4,128)}, u32[]{:S(2)}) copy-start(f32[3,128]{1,0:T(4,128)} %param.17) | copy-start | bytes 4612
  13.3 2.3 %copy-start.14 = (f32[3,3,128]{2,1,0:T(4,128)S(1)}, f32[3,3,128]{2,1,0:T(4,128)}, u32[]{:S(2)}) copy-start(f32[3,3,128]{2,1,0:T(4,128)} %param.18) | copy-start | bytes 13828
  13.6 7.0 %collective-permute-start = (bf16[2,3,128]{2,0,1:T(2,128)(2,1)S(1)}, bf16[2,3,128]{2,0,1:T(2,128)(2,1)S(1)}, u32[]{:S(2)}, u32[]{:S(2)}) collective-permute-start(bf16[2,3,128]{2,0,1:T(2,128)(2,1)S(1)} %slice.63), channel_id=1, source_target_pairs={{0,4},{4,8},{8,12},{12,16},{16,20},{20,24},{24,28},{28,32},{32,36}... | collective-permute-start | bytes 4616 | tf_op jit(solution)/shard_map/ppermute | solution.py:35
  20.7 0.7 copy-start.16
  21.5 18.6 %copy-start.10 = (f32[2,1,2,256,128]{4,3,2,1,0:T(8,128)S(1)}, f32[2,1,2,256,128]{4,3,2,1,0:T(8,128)}, u32[]{:S(2)}) copy-start(f32[2,1,2,256,128]{4,3,2,1,0:T(8,128)} %param.20) | copy-start | bytes 1572868
  22.4 34.8 %all-to-all-start.1 = ((bf16[2,1,256,128]{2,0,1,3:T(2,128)(2,1)}), bf16[2,1,256,128]{2,0,1,3:T(2,128)(2,1)S(1)}, u32[]{:S(2)}, u32[]{:S(2)}) async-start(bf16[2,1,256,128]{2,0,1,3:T(2,128)(2,1)} %copy.33), calls=%async_computation.1 | async-start | bytes 262144 | tf_op jit(solution)/shard_map/all_to_all | solution.py:135
  57.2 39.3 %all-to-all-start = ((f32[2,1,2,256,128]{3,2,1,0,4:T(2,128)}), f32[2,1,2,256,128]{3,2,1,0,4:T(2,128)S(1)}, u32[]{:S(2)}, u32[]{:S(2)}) async-start(f32[2,1,2,256,128]{3,2,1,0,4:T(2,128)} %copy.31), calls=%async_computation | async-start | bytes 1048576 | tf_op jit(solution)/shard_map/all_to_all | solution.py:138
  63.3 0.7 copy-start.18
  64.6 0.9 copy-start.11
  64.6 1.2 copy-start.8
  65.5 1.0 copy-start.3
  65.5 1.0 copy-start.6
  65.8 1.0 copy-start.2
  66.8 0.9 copy-start.1
  66.8 1.0 copy-start.5
  67.8 1.1 copy-start.4
  96.8 1.0 copy-start.7
  100.3 0.9 copy-start.9
  101.2 0.9 copy-start.12
  105.7 21.1 %all-to-all-start.2 = ((bf16[128,2,128]{2,1,0:T(2,128)(2,1)}), bf16[128,2,128]{2,1,0:T(2,128)(2,1)S(1)}, u32[]{:S(2)}, u32[]{:S(2)}) async-start(bf16[128,2,128]{2,1,0:T(2,128)(2,1)} %reshape.54), calls=%async_computation.2 | async-start | bytes 131072 | tf_op jit(solution)/shard_map/all_to_all | solution.py:144
  126.9 7.4 %collective-permute-start.1 = (bf16[256,128]{0,1:T(8,128)(2,1)S(1)}, bf16[256,128]{0,1:T(8,128)(2,1)S(1)}, u32[]{:S(2)}, u32[]{:S(2)}) collective-permute-start(bf16[256,128]{0,1:T(8,128)(2,1)S(1)} %get-tuple-element.6), channel_id=1, source_target_pairs={{0,1},{1,2},{2,3},{3,0},{4,5},{5,6},{6,7},{7,4},{8,9},{9,10},{10,1... | collective-permute-start | bytes 196616 | tf_op jit(solution)/shard_map/ppermute | solution.py:20
  130.6 6.2 %collective-permute-start.2 = (bf16[256,128]{0,1:T(8,128)(2,1)S(1)}, bf16[256,128]{0,1:T(8,128)(2,1)S(1)}, u32[]{:S(2)}, u32[]{:S(2)}) collective-permute-start(bf16[256,128]{0,1:T(8,128)(2,1)S(1)} %get-tuple-element.6), channel_id=1, source_target_pairs={{0,3},{1,0},{2,1},{3,2},{4,7},{5,4},{6,5},{7,6},{8,11},{9,8},{10,9... | collective-permute-start | bytes 196616 | tf_op jit(solution)/shard_map/ppermute | solution.py:25
  134.3 7.4 %collective-permute-start.3 = (bf16[256,128]{0,1:T(8,128)(2,1)S(1)}, bf16[256,128]{0,1:T(8,128)(2,1)S(1)}, u32[]{:S(2)}, u32[]{:S(2)}) collective-permute-start(bf16[256,128]{0,1:T(8,128)(2,1)S(1)} %collective-permute-done.1), channel_id=1, source_target_pairs={{0,1},{1,2},{2,3},{3,0},{4,5},{5,6},{6,7},{7,4},{8,9},{9,10},{10,1... | collective-permute-start | bytes 196616 | tf_op jit(solution)/shard_map/ppermute | solution.py:20
  136.8 4.9 %copy-start.17 = (f32[128]{0:T(128)S(1)}, f32[128]{0:T(128)}, u32[]{:S(2)}) copy-start(f32[128]{0:T(128)} %param.23) | copy-start | bytes 1540
